TPU v7x, 32 devices: a whole 2x2x4 slice. The times are simulated.
32 devices in a mesh: section: 2 (over x), seq: 8 (over z, y), head: 2 (over core).
Axes of the slice: x: 2, y: 2, z: 4, core: 2. Of those that a mesh axis runs over, the one named last changes fastest.
Arguments:
- bwd_input: bfloat16 [2, 1024, 3584], P('section', 'seq', 'head'), may hold values from -6 to 6
- bwd_docs: int32 [2, 1024], P('section', 'seq'), may hold values from 0 to 3, as said below
- bwd_grad: bfloat16 [2, 1024, 3584], P('section', 'seq', 'head'), may hold values from -6 to 6
- proj_weight: bfloat16 [2, 256, 3584], P('section', 'seq', 'head'), may hold values from -0.09375 to 0.09375
- step_weight: float32 [2, 3584], P('section', 'head'), may hold values from -0.75 to 0.75
- step_bias: float32 [2, 56], P('section', 'head'), may hold values from -5 to -2
- rate_log: float32 [2, 56], P('section', 'head'), may hold values from -4 to 0.5
- skip_gain: float32 [2, 56], P('section', 'head'), may hold values from 0.5 to 1.5
Outputs:
- prev_grad: bfloat16 [2, 1024, 3584], P('section', 'seq', 'head')
- grad_proj: float32 [2, 256, 3584], P('section', 'seq', 'head')
- grad_step_weight: float32 [2, 3584], P('section', 'head')
- grad_step_bias: float32 [2, 56], P('section', 'head')
- grad_rate_log: float32 [2, 56], P('section', 'head')
- grad_skip: float32 [2, 56], P('section', 'head')
Inputs may be any that keep to these rules, and one draw needn't show every extreme that they name: `bwd_docs`: document ids of each row never fall, start at 0, every id occurs, and one document of each row holds 512 tokens.
All inputs are finite; a program needn't handle non-finite values.
Results may differ from a plain program's by a relative error of at most 0.023.
Values may be sent and summed in bfloat16 or wider, within the bound.
No kernel may reach another device: no remote copies, remote signals or barrier semaphores. Data moves between devices by JAX's collectives and lax.ppermute only.
A program may use at most 64 MiB of HBM per device.

v0:
```python
import jax
import jax.numpy as jnp
from jax import lax
from jax.sharding import PartitionSpec as P

EXACT = lax.Precision.HIGHEST


def shifted(block, axis, distance):
    devices = range(lax.axis_size(axis))
    route = [(i - distance, i) for i in devices if i - distance in devices]
    return lax.ppermute(block, axis, route)


def entering(value, axis, combine, identity):
    size, mine = (lax.axis_size(axis), lax.axis_index(axis))
    everything = jax.tree.map(
        lambda part, kind: lax.all_gather(part.astype(kind), axis),
        value,
        (jnp.bfloat16, jnp.bfloat16),
    )
    start = jax.tree.map(
        lambda part, zero: jnp.broadcast_to(jnp.asarray(zero, part.dtype), part.shape),
        value,
        identity,
    )

    def lap(k, before):
        reached = k < mine
        new = combine(
            before, jax.tree.map(lambda part, own: part[k].astype(own.dtype), everything, value)
        )
        return jax.tree.map(lambda a, b: jnp.where(reached, a, b), new, before)

    return lax.fori_loop(0, size, lap, start)


def entering_2(value, axis, combine, identity):
    size, mine = (lax.axis_size(axis), lax.axis_index(axis))
    everything = jax.tree.map(
        lambda part, kind: lax.all_gather(part.astype(kind), axis),
        value,
        jax.tree.map(lambda a: jnp.bfloat16 if a.dtype == jnp.float32 else a.dtype, value),
    )
    start = jax.tree.map(
        lambda part, zero: jnp.broadcast_to(jnp.asarray(zero, part.dtype), part.shape),
        value,
        identity,
    )

    def lap(k, before):
        at = size - 1 - k
        reached = at > mine
        new = combine(
            before, jax.tree.map(lambda part, own: part[at].astype(own.dtype), everything, value)
        )
        return jax.tree.map(lambda a, b: jnp.where(reached, a, b), new, before)

    return lax.fori_loop(0, size, lap, start)


def contract(spec, left, right):
    return jnp.einsum(spec, left, right, preferred_element_type=jnp.float32)


def local_setup(values, step_weight, step_bias, rate_log):
    tokens = values.shape[0]
    raw_step = (
        jnp.einsum("thp,hp->th", values.astype(jnp.float32), step_weight, precision=EXACT)
        + step_bias[None, :]
    )
    step_size = jax.nn.softplus(raw_step)
    decay_log = -jnp.exp(rate_log)[None, :] * step_size
    row_ids = lax.broadcasted_iota(jnp.int32, (tokens, tokens), 0)
    col_ids = lax.broadcasted_iota(jnp.int32, (tokens, tokens), 1)
    triangle = (row_ids >= col_ids).astype(jnp.float32)
    cumulative = jnp.dot(triangle, decay_log, precision=EXACT)
    return (step_size, cumulative, row_ids, col_ids)


def span_summary(values, mixer, step_weight, step_bias, rate_log, docs, doc_before):
    step_size, cumulative, row_ids, col_ids = local_setup(values, step_weight, step_bias, rate_log)
    final_log = cumulative[-1]
    tail_mask = (docs == docs[-1]).astype(jnp.float32)[:, None]
    tail_weight = (
        jnp.exp(jnp.where(tail_mask > 0, final_log[None, :] - cumulative, 0.0))
        * tail_mask
        * step_size
    )
    unbroken = (docs[-1] == doc_before).astype(jnp.float32)
    carry_decay = jnp.exp(final_log) * unbroken
    half_width = mixer.shape[1] // 2
    writers = mixer[:, :half_width]
    weighted = (tail_weight[:, :, None] * writers.astype(jnp.float32)[:, None, :]).astype(
        jnp.bfloat16
    )
    span_state = contract("thn,thp->hnp", weighted, values)
    return (carry_decay, span_state)


def span_output(
    values, mixer, step_weight, step_bias, rate_log, skip_gain, docs, doc_before, incoming
):
    step_size, cumulative, row_ids, col_ids = local_setup(values, step_weight, step_bias, rate_log)
    half_width = mixer.shape[1] // 2
    writers = mixer[:, :half_width]
    readers = mixer[:, half_width:]
    affinity = jnp.dot(readers, writers.T, preferred_element_type=jnp.float32)
    same_doc = ((docs[:, None] == docs[None, :]) & (row_ids >= col_ids)).astype(jnp.float32)
    heads_first = cumulative.T
    log_gap = heads_first[:, :, None] - heads_first[:, None, :]
    mixing = (
        jnp.exp(jnp.where(same_doc[None] > 0, log_gap, 0.0))
        * same_doc[None]
        * affinity[None]
        * step_size.T[:, None, :]
    )
    mixing = mixing.astype(jnp.bfloat16)
    local_part = contract("hts,shp->thp", mixing, values)
    unbroken = (docs == doc_before).astype(jnp.float32)
    carry_scale = jnp.exp(cumulative) * unbroken[:, None]
    carried = jnp.einsum("tn,hnp->thp", readers.astype(jnp.float32), incoming, precision=EXACT)
    combined = (
        values.astype(jnp.float32) * (1.0 + skip_gain)[None, :, None]
        + local_part
        + carry_scale[:, :, None] * carried
    )
    return combined.astype(jnp.bfloat16)


def carry_join(earlier, later):
    return (earlier[0] * later[0], later[0][:, None] * earlier[1] + later[1])


def back_join(earlier, later):
    return (earlier[0] * later[0], later[1] + later[0][:, None] * earlier[1])


def shards(bwd_input, bwd_docs, bwd_grad, proj_weight, step_weight, step_bias, rate_log, skip_gain):
    tokens = bwd_input.shape[1]
    channels_here = bwd_input.shape[2]
    heads_here = step_bias.shape[1]
    head_width = channels_here // heads_here
    bwd_flat = bwd_input[0]
    bwd_values = bwd_flat.reshape(tokens, heads_here, head_width)
    weight_heads = step_weight[0].reshape(heads_here, head_width)
    bias_heads = step_bias[0]
    rate_heads = rate_log[0]
    skip_heads = skip_gain[0]
    docs_bwd = bwd_docs[0]
    doc_before = shifted(docs_bwd[-1:], "seq", 1)[0]
    full_weight = lax.all_gather(proj_weight[0], "seq", axis=0, tiled=True)
    partial_value = jnp.dot(bwd_flat, full_weight.T, preferred_element_type=jnp.float32)
    mixer_bwd = lax.psum_scatter(
        partial_value.astype(jnp.bfloat16), "head", scatter_dimension=1, tiled=True
    )

    def summary_bwd(values_in, mixer_in, weight_in, bias_in, rate_in):
        return span_summary(values_in, mixer_in, weight_in, bias_in, rate_in, docs_bwd, doc_before)

    summary_out, summary_pull = jax.vjp(
        summary_bwd, bwd_values, mixer_bwd, weight_heads, bias_heads, rate_heads
    )
    decay_bwd, state_bwd = summary_out
    state_shape = state_bwd.shape
    state_flat = state_bwd.reshape(heads_here, -1)
    seeds = (jnp.ones_like(decay_bwd), jnp.zeros_like(state_flat))
    incoming_flat = entering((decay_bwd, state_flat), "seq", carry_join, seeds)[1]
    incoming_bwd = incoming_flat.reshape(state_shape)

    def output_bwd(values_in, mixer_in, weight_in, bias_in, rate_in, skip_in, state_in):
        return span_output(
            values_in,
            mixer_in,
            weight_in,
            bias_in,
            rate_in,
            skip_in,
            docs_bwd,
            doc_before,
            state_in,
        )

    unused, output_pull = jax.vjp(
        output_bwd,
        bwd_values,
        mixer_bwd,
        weight_heads,
        bias_heads,
        rate_heads,
        skip_heads,
        incoming_bwd,
    )
    cotangent = bwd_grad[0].reshape(tokens, heads_here, head_width)
    out_grads = output_pull(cotangent)
    state_grad = out_grads[6].reshape(heads_here, -1)
    back_seeds = (jnp.ones_like(decay_bwd), jnp.zeros_like(state_grad))
    adjoint_flat = entering_2((decay_bwd, state_grad), "seq", back_join, back_seeds)[1]
    decay_grad = jnp.sum(adjoint_flat * incoming_flat, axis=1)
    sum_grads = summary_pull((decay_grad, adjoint_flat.reshape(state_shape)))
    mixer_grad = (out_grads[1].astype(jnp.float32) + sum_grads[1].astype(jnp.float32)).astype(
        jnp.bfloat16
    )
    mixer_full = lax.all_gather(mixer_grad, "head", axis=1, tiled=True)
    back_proj = jnp.dot(mixer_full, full_weight, preferred_element_type=jnp.float32)
    value_grad = (out_grads[0].astype(jnp.float32) + sum_grads[0].astype(jnp.float32)).reshape(
        tokens, channels_here
    ) + back_proj
    value_grad = value_grad.astype(jnp.bfloat16)
    prev_part = shifted(value_grad.reshape(1, tokens, channels_here), "section", -1)
    grad_rows = lax.psum_scatter(
        lax.dot_general(
            mixer_full, bwd_flat, (((0,), (0,)), ((), ())), preferred_element_type=jnp.float32
        ).astype(jnp.bfloat16),
        "seq",
        scatter_dimension=0,
        tiled=True,
    ).astype(jnp.float32)
    totals = lax.psum(
        (
            (out_grads[2] + sum_grads[2]).reshape(channels_here),
            out_grads[3] + sum_grads[3],
            out_grads[4] + sum_grads[4],
            out_grads[5],
        ),
        "seq",
    )
    return (
        prev_part,
        grad_rows[None],
        totals[0][None],
        totals[1][None],
        totals[2][None],
        totals[3][None],
    )


def solution(mesh):
    in_specs = (
        P("section", "seq", "head"),
        P("section", "seq"),
        P("section", "seq", "head"),
        P("section", "seq", "head"),
        P("section", "head"),
        P("section", "head"),
        P("section", "head"),
        P("section", "head"),
    )
    out_specs = (
        P("section", "seq", "head"),
        P("section", "seq", "head"),
        P("section", "head"),
        P("section", "head"),
        P("section", "head"),
        P("section", "head"),
    )
    return jax.shard_map(shards, mesh=mesh, in_specs=in_specs, out_specs=out_specs, check_vma=False)
```

profile of v0, /device:TPU:0, one launch (start us, length us, event | category | flops | bytes accessed | tf_op | source)
XLA Modules:
  0.0 258.4 jit_solution(6643911628214129203)
XLA Ops:
  7.2 1.3 slice.21
  8.5 5.4 %collective-permute-start = (s32[1]{0:T(128)}, s32[1]{0:T(128)}, u32[]{:S(2)}, u32[]{:S(2)}) collective-permute-start(s32[1]{0:T(128)} %bitcast.17), channel_id=1, source_target_pairs={{0,2},{2,4},{4,6},{6,8},{8,10},{10,12},{12,14},{1,3},{3,5},{5,7},{... | collective-permute-start | bytes 20 | tf_op jit(solution)/shard_map/ppermute | solution.py:12
  13.9 32.6 %all-gather = bf16[1,256,1792]{2,1,0:T(8,128)(2,1)S(1)} all-gather(bf16[1,32,1792]{2,1,0:T(8,128)(2,1)} %param.16), channel_id=2, replica_groups=mesh['section'=2,'seq'=8,'head'=2] {'seq'}, dimensions={1}, use_global_device_ids=true | all-gather | bytes 1032192 | tf_op jit(solution)/shard_map/all_gather | solution.py:152
  46.5 1.5 convolution_convert_fusion.7
  48.0 0.7 copy.113
  51.1 1.2 broadcast_compare_fusion.1
  52.4 0.9 exponential_multiply_fusion
  54.0 1.1 reduce-scatter.7.cloned.1.call-done
  55.2 0.7 slice_convert_fusion
  56.3 1.1 convert_element_type.239
  58.4 1.3 add_bitcast_fusion.1
  59.6 1.4 broadcast_compare_fusion
  61.1 20.8 %all-gather.1 = bf16[8,1,28]{2,1,0:T(2,128)(2,1)S(1)} all-gather(bf16[1,1,28]{2,1,0:T(2,128)(2,1)} %get-tuple-element.322), channel_id=1, replica_groups=mesh['section'=2,'seq'=8,'head'=2] {'seq'}, dimensions={0}, use_global_device_ids=true | all-gather | bytes 504 | tf_op jit(solution)/shard_map/all_gather | solution.py:18
  82.5 1.9 fusion.28
  85.9 1.1 convert_element_type.246
  87.0 0.8 fusion.75
  87.9 20.1 %all-gather.5.cloned.1.call-done = bf16[8,28,4096]{2,1,0:T(8,128)(2,1)} async-done(((bf16[1,28,4096]{2,1,0:T(8,128)(2,1)}), bf16[8,28,4096]{2,1,0:T(8,128)(2,1)}) %all-gather.5.cloned.1.call-update) | async-done | bytes 1835024 | tf_op jit(solution)/shard_map/all_gather | solution.py:18
  108.0 14.4 %while.30 = (s32[]{:T(128)}, f32[28,4096]{1,0:T(8,128)S(1)}, s32[]{:T(128)}, bf16[8,28]{1,0:T(8,128)(2,1)}, bf16[8,28,4096]{2,1,0:T(8,128)(2,1)}, /*index=5*/s32[]{:T(128)}, s32[]{:T(128)}) while((s32[]{:T(128)}, f32[28,4096]{1,0:T(8,128)S(1)}, s32[]{:T(128)}, bf16[8,28]{1,0:T(8,128)(2,1)}, bf16[8,28,4096]{2,1,0:T(8,128)(2,1)}, ...), condition=%wide.region_3.5_spmd.clone, body=%wide.region_2.4_spmd.clone.sunk | while | flops 573472 | bytes 1147273 | solution.py:35
  108.6 1.1 fusion.116
  109.8 0.7 bitcast_convert_fusion.5
  110.5 1.1 fusion.116
  112.3 1.1 fusion.116
  114.1 1.1 fusion.116
  115.2 0.7 bitcast_convert_fusion.5
  115.9 1.1 fusion.116
  117.0 0.7 bitcast_convert_fusion.5
  117.7 1.1 fusion.116
  119.5 1.1 fusion.116
  121.3 1.1 fusion.116
  122.4 36.1 %all-gather.7.cloned.1.call-done = bf16[8,28,4096]{2,1,0:T(8,128)(2,1)} async-done(((bf16[1,28,4096]{2,1,0:T(8,128)(2,1)}), bf16[8,28,4096]{2,1,0:T(8,128)(2,1)}) %all-gather.7.cloned.1.call-update) | async-done | bytes 1835024 | tf_op jit(solution)/shard_map/all_gather | solution.py:41
  158.5 14.4 %while.31 = (s32[]{:T(128)}, f32[28,4096]{1,0:T(8,128)S(1)}, s32[]{:T(128)}, bf16[8,28,4096]{2,1,0:T(8,128)(2,1)}, bf16[8,28]{1,0:T(8,128)(2,1)}, /*index=5*/s32[]{:T(128)}, s32[]{:T(128)}, s32[]{:T(128)}, s32[]{:T(128)}) while((s32[]{:T(128)}, f32[28,4096]{1,0:T(8,128)S(1)}, s32[]{:T(128)}, bf16[8,28,4096]{2,1,0:T(8,128)(2,1)}, ...), condition=%wide.region_8.10_spmd.clone, body=%wide.region_7.9_spmd.clone.sunk | while | flops 573476 | bytes 1147335 | solution.py:59
  159.2 1.1 fusion.117
  160.3 0.7 bitcast_convert_fusion.6
  161.0 1.1 fusion.117
  162.1 0.7 bitcast_convert_fusion.6
  162.8 1.1 fusion.117
  163.9 0.7 bitcast_convert_fusion.6
  164.6 1.1 fusion.117
  165.7 0.7 bitcast_convert_fusion.6
  166.4 1.1 fusion.117
  167.5 0.7 bitcast_convert_fusion.6
  168.2 1.1 fusion.117
  169.3 0.7 bitcast_convert_fusion.6
  170.0 1.1 fusion.117
  171.1 0.7 bitcast_convert_fusion.6
  171.8 1.1 fusion.117
  172.9 1.2 reshape.241
  175.2 1.5 multiply_reduce_fusion
  176.8 0.8 fusion.90
  177.8 1.9 fusion.14
  179.9 1.2 copy.90
  181.1 2.3 fusion.26
  184.4 2.0 all_gather.24
  186.4 1.3 convolution_convert_fusion
  188.7 0.9 fusion.24
  190.2 1.3 copy.100
  191.5 1.5 fusion.3
  193.0 1.3 collective-permute-start.1
  194.3 0.8 fusion.92
  195.1 0.8 fusion.93
  196.1 20.1 %all-reduce.4 = (f32[1,1792]{1,0:T(1,128)}, f32[1,28]{1,0:T(1,128)}, f32[1,28]{1,0:T(1,128)}, f32[1,28]{1,0:T(1,128)}) all-reduce(f32[1,1792]{1,0:T(1,128)S(1)} %broadcast_in_dim.73, f32[1,28]{1,0:T(1,128)S(1)} %get-tuple-element.329, f32[1,28]{1,0:T(1,128)S(1)} %get-tuple-element.328, ...), channel_id=1, replica_groups=mesh['section'=2,'seq'=8,'head'=2] {'seq'}, use_global_device_ids=true, to_apply=%region_15.17 | all-reduce | flops 1876 | bytes 15008 | tf_op jit(solution)/shard_map/psum | solution.py:219
  216.2 33.3 %reduce-scatter.5.cloned.1.call-done = bf16[32,1792]{1,0:T(8,128)(2,1)} async-done(((bf16[256,1792]{1,0:T(8,128)(2,1)}), bf16[32,1792]{1,0:T(8,128)(2,1)}) %reduce-scatter.5.cloned.1.call-update) | async-done | bytes 114704 | tf_op jit(solution)/shard_map/reduce_scatter | solution.py:211
  249.5 1.6 bitcast_convert_fusion.2
  251.1 0.8 copy.133
  (125 shorter events, 13.5 us)
Async XLA Ops:
  7.2 41.7 %copy-start = (bf16[1,128,1792]{2,1,0:T(8,128)(2,1)S(1)}, bf16[1,128,1792]{2,1,0:T(8,128)(2,1)}, u32[]{:S(2)}) copy-start(bf16[1,128,1792]{2,1,0:T(8,128)(2,1)} %param.13) | copy-start | bytes 1376260
  7.2 41.9 %copy-start.27 = (f32[1,28]{1,0:T(1,128)S(1)}, f32[1,28]{1,0:T(1,128)}, u32[]{:S(2)}) copy-start(f32[1,28]{1,0:T(1,128)} %param.19) | copy-start | bytes 340
  7.2 42.0 %copy-start.15 = (f32[1,1792]{1,0:T(1,128)S(1)}, f32[1,1792]{1,0:T(1,128)}, u32[]{:S(2)}) copy-start(f32[1,1792]{1,0:T(1,128)} %param.17) | copy-start | bytes 21508
  7.2 48.0 %reduce-scatter.7.cloned.1.call-start = ((), (), s32[]{:S(2)}) async-start(), calls=%async_computation.5 | async-start | bytes 98304
  8.5 41.3 %collective-permute-start = (s32[1]{0:T(128)}, s32[1]{0:T(128)}, u32[]{:S(2)}, u32[]{:S(2)}) collective-permute-start(s32[1]{0:T(128)} %bitcast.17), channel_id=1, source_target_pairs={{0,2},{2,4},{4,6},{6,8},{8,10},{10,12},{12,14},{1,3},{3,5},{5,7},{... | collective-permute-start | bytes 20 | tf_op jit(solution)/shard_map/ppermute | solution.py:12
  46.5 4.6 %copy-start.22 = (s32[1,128]{1,0:T(1,128)S(1)}, s32[1,128]{1,0:T(1,128)}, u32[]{:S(2)}) copy-start(s32[1,128]{1,0:T(1,128)} %param.14) | copy-start | bytes 1540
  46.5 5.8 %copy-start.23 = (f32[1,28]{1,0:T(1,128)S(1)}, f32[1,28]{1,0:T(1,128)}, u32[]{:S(2)}) copy-start(f32[1,28]{1,0:T(1,128)} %param.18) | copy-start | bytes 340
  48.8 59.2 %all-gather.5.cloned.1.call-start = ((), (), s32[]{:S(2)}) async-start(), calls=%async_computation.2 | async-start | bytes 2359296 | tf_op jit(solution)/shard_map/all_gather | solution.py:18
  49.1 33.3 %copy-start.2 = (bf16[1,128,1792]{1,2,0:T(8,128)(2,1)}, bf16[1,128,1792]{1,2,0:T(8,128)(2,1)S(1)}, u32[]{:S(2)}) copy-start(bf16[1,128,1792]{1,2,0:T(8,128)(2,1)S(1)} %copy.82) | copy-start | bytes 1376260
  49.1 9.0 %copy-start.6 = (bf16[1,128,1792]{2,1,0:T(8,128)(2,1)S(1)}, bf16[1,128,1792]{2,1,0:T(8,128)(2,1)}, u32[]{:S(2)}) copy-start(bf16[1,128,1792]{2,1,0:T(8,128)(2,1)} %param.15) | copy-start | bytes 1376260
  49.2 4.1 %copy-start.31 = (f32[28]{0:T(128)}, f32[28]{0:T(128)S(1)}, u32[]{:S(2)}) copy-start(f32[28]{0:T(128)S(1)} %negate_bitcast_fusion) | copy-start | bytes 340
  52.3 0.9 copy-start.29
  52.3 2.8 %copy-start.16 = (pred[128]{0:T(512)(128)(4,1)}, pred[128]{0:T(512)(128)(4,1)S(1)}, u32[]{:S(2)}) copy-start(pred[128]{0:T(512)(128)(4,1)S(1)} %get-tuple-element.312) | copy-start | bytes 388
  52.3 2.8 %copy-start.18 = (f32[128]{0:T(128)}, f32[128]{0:T(128)S(1)}, u32[]{:S(2)}) copy-start(f32[128]{0:T(128)S(1)} %get-tuple-element.313) | copy-start | bytes 1540
  53.2 0.6 copy-start.12
  53.9 1.3 copy-start.20
  56.3 28.8 %copy-start.7 = (bf16[128,128]{1,0:T(8,128)(2,1)S(1)}, bf16[128,128]{1,0:T(8,128)(2,1)}, u32[]{:S(2)}) copy-start(bf16[128,128]{1,0:T(8,128)(2,1)} %reduce-scatter.7.cloned.1.call-done) | copy-start | bytes 98308
  57.4 101.1 %all-gather.7.cloned.1.call-start = ((), (), s32[]{:S(2)}) async-start(), calls=%async_computation.3 | async-start | bytes 2359296 | tf_op jit(solution)/shard_map/all_gather | solution.py:41
  58.4 26.7 %copy-start.9 = (f32[128,28]{0,1:T(8,128)S(1)}, f32[128,28]{0,1:T(8,128)}, u32[]{:S(2)}) copy-start(f32[128,28]{0,1:T(8,128)} %get-tuple-element.326) | copy-start | bytes 43012
  87.8 161.7 %reduce-scatter.5.cloned.1.call-start = ((), (), s32[]{:S(2)}) async-start(), calls=%async_computation.4 | async-start | bytes 1032192 | tf_op jit(solution)/shard_map/reduce_scatter | solution.py:211
  174.8 2.9 %copy-start.3 = (bf16[1,128,1792]{1,2,0:T(8,128)(2,1)S(1)}, bf16[1,128,1792]{1,2,0:T(8,128)(2,1)}, u32[]{:S(2)}) copy-start(bf16[1,128,1792]{1,2,0:T(8,128)(2,1)} %copy-done.2) | copy-start | bytes 1376260
  175.2 2.5 copy-start.10
  175.2 2.5 copy-start.11
  175.2 2.5 copy-start.13
  175.2 2.5 copy-start.14
  181.1 2.4 copy-start.4
  183.4 3.0 %copy-start.1 = (bf16[1,128,1792]{2,1,0:T(8,128)(2,1)S(1)}, bf16[1,128,1792]{2,1,0:T(8,128)(2,1)}, u32[]{:S(2)}) copy-start(bf16[1,128,1792]{2,1,0:T(8,128)(2,1)} %param.13) | copy-start | bytes 1376260
  184.1 3.6 %copy-start.25 = (f32[28]{0:T(128)S(1)}, f32[28]{0:T(128)}, u32[]{:S(2)}) copy-start(f32[28]{0:T(128)} %multiply_reduce_fusion.2) | copy-start | bytes 340
  184.1 3.9 %copy-start.17 = (pred[128]{0:T(512)(128)(4,1)S(1)}, pred[128]{0:T(512)(128)(4,1)}, u32[]{:S(2)}) copy-start(pred[128]{0:T(512)(128)(4,1)} %copy-done.16) | copy-start | bytes 388
  184.1 3.9 %copy-start.19 = (f32[128]{0:T(128)S(1)}, f32[128]{0:T(128)}, u32[]{:S(2)}) copy-start(f32[128]{0:T(128)} %copy-done.18) | copy-start | bytes 1540
  184.2 3.9 %copy-start.21 = (f32[28]{0:T(128)S(1)}, f32[28]{0:T(128)}, u32[]{:S(2)}) copy-start(f32[28]{0:T(128)} %copy-done.20) | copy-start | bytes 340
  184.2 3.9 %copy-start.24 = (f32[1,28]{1,0:T(1,128)S(1)}, f32[1,28]{1,0:T(1,128)}, u32[]{:S(2)}) copy-start(f32[1,28]{1,0:T(1,128)} %param.18) | copy-start | bytes 340
  184.2 3.9 %copy-start.30 = (f32[128]{0:T(128)S(1)}, f32[128]{0:T(128)}, u32[]{:S(2)}) copy-start(f32[128]{0:T(128)} %copy-done.29) | copy-start | bytes 1540
  184.2 3.9 %copy-start.32 = (f32[28]{0:T(128)S(1)}, f32[28]{0:T(128)}, u32[]{:S(2)}) copy-start(f32[28]{0:T(128)} %copy-done.31) | copy-start | bytes 340
  184.4 4.4 %copy-start.8 = (f32[28,64]{1,0:T(8,128)S(1)}, f32[28,64]{1,0:T(8,128)}, u32[]{:S(2)}) copy-start(f32[28,64]{1,0:T(8,128)} %reshape_squeeze.10) | copy-start | bytes 21508
  184.4 4.4 %copy-start.33 = (f32[28]{0:T(128)S(1)}, f32[28]{0:T(128)}, u32[]{:S(2)}) copy-start(f32[28]{0:T(128)} %add_bitcast_fusion.1) | copy-start | bytes 340
  188.7 1.0 copy-start.5
  191.5 4.5 %copy-start.28 = (f32[1,28]{1,0:T(1,128)S(1)}, f32[1,28]{1,0:T(1,128)}, u32[]{:S(2)}) copy-start(f32[1,28]{1,0:T(1,128)} %param.19) | copy-start | bytes 340
  191.5 4.6 %copy-start.26 = (f32[28]{0:T(128)S(1)}, f32[28]{0:T(128)}, u32[]{:S(2)}) copy-start(f32[28]{0:T(128)} %reduce_sum.161) | copy-start | bytes 340
  193.0 23.2 %collective-permute-start.1 = (bf16[1,128,1792]{2,1,0:T(8,128)(2,1)S(1)}, bf16[1,128,1792]{2,1,0:T(8,128)(2,1)S(1)}, u32[]{:S(2)}, u32[]{:S(2)}) collective-permute-start(bf16[1,128,1792]{2,1,0:T(8,128)(2,1)S(1)} %fusion.3), channel_id=1, source_target_pairs={{16,0},{17,1},{18,2},{19,3},{20,4},{21,5},{22,6},{23,7},{24,8},{25... | collective-permute-start | bytes 1376264 | tf_op jit(solution)/shard_map/ppermute | solution.py:12
Sparse Core Ops, SparseCore 0:
  48.9 6.2 reduce-scatter.6
  57.5 50.4 all-gather.4
  110.7 47.7 all-gather.6
  187.9 61.6 reduce-scatter.4
where the time goes:
time: 260 us; the launch traced here: 258 us
  waiting for transfers between devices  90.7 us (35%)
  blocking collectives  75.6 us (29%)
  other arithmetic  39.5 us (15%)
  matrix products  17.4 us (7%)
  between operations  15.5 us (6%)
  local copies, waits for them, and re-layouts  12.4 us (5%)
  starting transfers between devices  6.82 us (3%)
    all_gather x1, waiting for transfers between devices, entering_2(): lax.all_gather(part.astype(kind), axis)  36.1 us
    reduce_scatter x1, waiting for transfers between devices, shards(): lax.psum_scatter(lax.dot_general(mixer_full, bwd_flat, (((0,), (0,)), (()...  33.3 us
    all_gather x1, blocking collectives, shards(): full_weight = lax.all_gather(proj_weight[0], 'seq', axis=0, tiled=True)  32.6 us
    all_gather x1, blocking collectives, entering(): lax.all_gather(part.astype(kind), axis)  20.8 us
    psum x1, blocking collectives, shards(): lax.psum(((out_grads[2] + sum_grads[2]).reshape(channels_here), out_grads...  20.1 us
    all_gather x1, waiting for transfers between devices, entering(): lax.all_gather(part.astype(kind), axis)  20.1 us
    select_n x16, other arithmetic, lap(): return jax.tree.map(lambda a, b: jnp.where(reached, a, b), new, before)  17.4 us
    ppermute x2, starting transfers between devices, shifted(): return lax.ppermute(block, axis, route)  6.65 us
  transfers between devices with their start and end apart: 6, of which 4 were waited for; matrix products, arithmetic and copies ran while one was open for 14% of the time, Pallas kernels for 0%

commit v1 on v0

--- a/solution.py
+++ b/solution.py
@@ -149,7 +149,14 @@
     skip_heads = skip_gain[0]
     docs_bwd = bwd_docs[0]
     doc_before = shifted(docs_bwd[-1:], "seq", 1)[0]
-    full_weight = lax.all_gather(proj_weight[0], "seq", axis=0, tiled=True)
+    ways, here = (lax.axis_size("seq"), lax.axis_index("seq"))
+    full_weight, reach = (proj_weight[0], 1)
+    while reach < ways:
+        theirs = lax.ppermute(full_weight, "seq", [(d, d ^ reach) for d in range(ways)])
+        mine_first = jnp.concatenate([full_weight, theirs], axis=0)
+        theirs_first = jnp.concatenate([theirs, full_weight], axis=0)
+        full_weight = jnp.where(here & reach == 0, mine_first, theirs_first)
+        reach = 2 * reach
     partial_value = jnp.dot(bwd_flat, full_weight.T, preferred_element_type=jnp.float32)
     mixer_bwd = lax.psum_scatter(
         partial_value.astype(jnp.bfloat16), "head", scatter_dimension=1, tiled=True

time: 260 us -> 250 us (0.962)
  blocking collectives: 75.6 us -> 42.9 us
  waiting for transfers between devices: 90.7 us -> 122 us
  other arithmetic: 39.5 us -> 25.6 us
  starting transfers between devices: 6.82 us -> 12.4 us
    all_gather x1 -> x0, blocking collectives: 32.6 us -> none  [shards(): full_weight = lax.all_gather(proj_weight[0], 'seq', axis=0, tiled=True)]
    ppermute x0 -> x3, waiting for transfers between devices: none -> 20.1 us  [shards(): lax.ppermute(full_weight, 'seq', [(d, d ^ reach) for d in range(ways)])]
    all_gather x1, waiting for transfers between devices: 20.1 us -> 39.6 us  [entering(): lax.all_gather(part.astype(kind), axis)]
    all_gather x1, waiting for transfers between devices: 36.1 us -> 21.8 us  [entering_2(): lax.all_gather(part.astype(kind), axis)]
    ppermute x0 -> x3, starting transfers between devices: none -> 7.05 us  [shards(): lax.ppermute(full_weight, 'seq', [(d, d ^ reach) for d in range(ways)])]
    reduce_scatter x0 -> x1, waiting for transfers between devices: none -> 6.54 us  [shards(): lax.psum_scatter(partial_value.astype(jnp.bfloat16), 'head', scatter_dime...]
    convert_element_type x8, other arithmetic: 5.52 us -> 0.06 us  [lap(): part[k].astype(own.dtype)]
    convert_element_type x8, other arithmetic: 5.52 us -> 0.06 us  [lap(): part[at].astype(own.dtype)]
  transfers between devices with their start and end apart: 6 -> 9, of which waited for: 4 -> 6; matrix products, arithmetic and copies ran while one was open for 14% -> 12% of each run, Pallas kernels for 0% -> 0%
where the time goes in v1:
time: 250 us; the launch traced here: 249 us
  waiting for transfers between devices  122 us (49%)
  blocking collectives  42.9 us (17%)
  other arithmetic  25.6 us (10%)
  matrix products  18.5 us (7%)
  between operations  15.4 us (6%)
  starting transfers between devices  12.4 us (5%)
  local copies, waits for them, and re-layouts  11.7 us (5%)
    all_gather x1, waiting for transfers between devices, entering(): lax.all_gather(part.astype(kind), axis)  39.6 us
    reduce_scatter x1, waiting for transfers between devices, shards(): lax.psum_scatter(lax.dot_general(mixer_full, bwd_flat, (((0,), (0,)), (()...  33.6 us
    all_gather x1, waiting for transfers between devices, entering_2(): lax.all_gather(part.astype(kind), axis)  21.8 us
    all_gather x1, blocking collectives, entering(): lax.all_gather(part.astype(kind), axis)  20.7 us
    psum x1, blocking collectives, shards(): lax.psum(((out_grads[2] + sum_grads[2]).reshape(channels_here), out_grads...  20.1 us
    ppermute x3, waiting for transfers between devices, shards(): lax.ppermute(full_weight, 'seq', [(d, d ^ reach) for d in range(ways)])  20.1 us
    select_n x16, other arithmetic, lap(): return jax.tree.map(lambda a, b: jnp.where(reached, a, b), new, before)  17.5 us
    ppermute x3, starting transfers between devices, shards(): lax.ppermute(full_weight, 'seq', [(d, d ^ reach) for d in range(ways)])  7.05 us
  transfers between devices with their start and end apart: 9, of which 6 were waited for; matrix products, arithmetic and copies ran while one was open for 12% of the time, Pallas kernels for 0%

profile of v1, /device:TPU:0, one launch (start us, length us, event | category | flops | bytes accessed | tf_op | source)
XLA Modules:
  0.0 248.8 jit_solution(1066373262604198638)
XLA Ops:
  7.2 3.0 %collective-permute-start = (bf16[32,1792]{1,0:T(8,128)(2,1)}, bf16[32,1792]{1,0:T(8,128)(2,1)S(1)}, u32[]{:S(2)}, u32[]{:S(2)}) collective-permute-start(bf16[32,1792]{1,0:T(8,128)(2,1)} %bitcast.251), channel_id=1, source_target_pairs={{0,2},{2,0},{4,6},{6,4},{8,10},{10,8},{12,14},{14,12},{1,3},{3,1},... | collective-permute-start | bytes 344072 | tf_op jit(solution)/shard_map/ppermute | solution.py:155
  10.3 3.3 %collective-permute-done = bf16[32,1792]{1,0:T(8,128)(2,1)S(1)} collective-permute-done((bf16[32,1792]{1,0:T(8,128)(2,1)}, bf16[32,1792]{1,0:T(8,128)(2,1)S(1)}, u32[]{:S(2)}, u32[]{:S(2)}) %collective-permute-start) | collective-permute-done | bytes 114720 | tf_op jit(solution)/shard_map/ppermute | solution.py:155
  13.6 1.0 maximum_select_fusion.2
  14.6 1.9 collective-permute-start.1
  16.5 1.2 slice.21
  17.7 3.9 %collective-permute-start.3 = (s32[1]{0:T(128)}, s32[1]{0:T(128)}, u32[]{:S(2)}, u32[]{:S(2)}) collective-permute-start(s32[1]{0:T(128)} %bitcast.18), channel_id=1, source_target_pairs={{0,2},{2,4},{4,6},{6,8},{8,10},{10,12},{12,14},{1,3},{3,5},{5,7},{... | collective-permute-start | bytes 20 | tf_op jit(solution)/shard_map/ppermute | solution.py:12
  21.7 0.7 reduce.2
  22.5 1.3 copy.72
  23.8 2.2 collective-permute-start.2
  26.0 0.5 fusion.92
  26.9 1.2 broadcast_compare_fusion.1
  28.2 16.7 %collective-permute-done.2 = bf16[128,1792]{1,0:T(8,128)(2,1)S(1)} collective-permute-done((bf16[128,1792]{1,0:T(8,128)(2,1)S(1)}, bf16[128,1792]{1,0:T(8,128)(2,1)S(1)}, u32[]{:S(2)}, u32[]{:S(2)}) %collective-permute-start.2) | collective-permute-done | bytes 458784 | tf_op jit(solution)/shard_map/ppermute | solution.py:155
  44.9 1.1 fusion.26
  46.3 6.5 %reduce-scatter.3.cloned.1.call-done = bf16[128,128]{0,1:T(8,128)(2,1)} async-done(((bf16[128,256]{0,1:T(8,128)(2,1)}), bf16[128,128]{0,1:T(8,128)(2,1)}) %reduce-scatter.3.cloned.1.call-update) | async-done | bytes 32784 | tf_op jit(solution)/shard_map/reduce_scatter | solution.py:161
  52.8 1.3 fusion.25
  54.4 1.1 convert_element_type.250
  55.6 0.5 add_bitcast_fusion.1
  56.1 0.7 broadcast_compare_fusion
  58.1 0.3 fusion.29
  58.7 20.7 %all-gather = bf16[8,1,28]{2,1,0:T(2,128)(2,1)S(1)} all-gather(bf16[1,1,28]{2,1,0:T(2,128)(2,1)S(1)} %get-tuple-element.322), channel_id=1, replica_groups=mesh['section'=2,'seq'=8,'head'=2] {'seq'}, dimensions={0}, use_global_device_ids=true | all-gather | bytes 504 | tf_op jit(solution)/shard_map/all_gather | solution.py:18
  79.5 0.7 reduce_sum.161
  80.1 1.1 convolution_convert_fusion.3
  81.3 2.1 convert_element_type.243
  83.5 0.8 fusion.74
  84.3 21.8 %all-gather.6.cloned.1.call-done = bf16[8,28,4096]{2,1,0:T(8,128)(2,1)} async-done(((bf16[1,28,4096]{2,1,0:T(8,128)(2,1)}), bf16[8,28,4096]{2,1,0:T(8,128)(2,1)}) %all-gather.6.cloned.1.call-update) | async-done | bytes 1835024 | tf_op jit(solution)/shard_map/all_gather | solution.py:41
  106.1 9.1 %while.31 = (s32[]{:T(128)}, f32[28,4096]{1,0:T(8,128)S(1)}, s32[]{:T(128)}, bf16[8,28,4096]{2,1,0:T(8,128)(2,1)}, bf16[8,28]{1,0:T(8,128)(2,1)S(1)}, /*index=5*/s32[]{:T(128)}, s32[]{:T(128)}, s32[]{:T(128)}, s32[]{:T(128)}) while((s32[]{:T(128)}, f32[28,4096]{1,0:T(8,128)S(1)}, s32[]{:T(128)}, bf16[8,28,4096]{2,1,0:T(8,128)(2,1)}, ...), condition=%wide.region_8.10_spmd.clone, body=%wide.region_7.9_spmd.clone.sunk | while | flops 573476 | bytes 1147335 | solution.py:59
  106.1 1.1 fusion.118
  107.3 1.1 fusion.118
  108.4 1.1 fusion.118
  109.5 1.1 fusion.118
  110.7 1.1 fusion.118
  111.8 1.1 fusion.118
  113.0 1.1 fusion.118
  114.1 1.1 fusion.118
  115.2 1.2 reshape.241
  116.4 39.6 %all-gather.4.cloned.1.call-done = bf16[8,28,4096]{2,1,0:T(8,128)(2,1)} async-done(((bf16[1,28,4096]{2,1,0:T(8,128)(2,1)}), bf16[8,28,4096]{2,1,0:T(8,128)(2,1)}) %all-gather.4.cloned.1.call-update) | async-done | bytes 1835024 | tf_op jit(solution)/shard_map/all_gather | solution.py:18
  156.1 9.0 %while.30 = (s32[]{:T(128)}, f32[28,4096]{1,0:T(8,128)S(1)}, s32[]{:T(128)}, bf16[8,28]{1,0:T(8,128)(2,1)S(1)}, bf16[8,28,4096]{2,1,0:T(8,128)(2,1)}, /*index=5*/s32[]{:T(128)}, s32[]{:T(128)}) while((s32[]{:T(128)}, f32[28,4096]{1,0:T(8,128)S(1)}, s32[]{:T(128)}, bf16[8,28]{1,0:T(8,128)(2,1)S(1)}, bf16[8,28,4096]{2,1,0:T(8,128)(2,1)}, ...), condition=%wide.region_3.5_spmd.clone, body=%wide.region_2.4_spmd.clone.sunk | while | flops 573472 | bytes 1147273 | solution.py:35
  156.1 1.1 fusion.117
  157.2 1.1 fusion.117
  158.3 1.1 fusion.117
  159.5 1.1 fusion.117
  160.6 1.1 fusion.117
  161.7 1.1 fusion.117
  162.9 1.1 fusion.117
  164.0 1.1 fusion.117
  165.1 0.7 multiply_reduce_fusion.2
  165.8 0.4 reshape.240
  166.2 1.4 multiply_reduce_fusion
  167.9 1.9 fusion.14
  169.9 1.2 copy.78
  171.1 1.7 fusion.78
  173.0 1.0 fusion.27
  174.3 2.0 all_gather.20
  176.4 1.3 convolution_convert_fusion
  178.5 0.9 fusion.24
  179.5 0.5 fusion.20
  180.5 2.4 fusion.3
  182.9 1.3 collective-permute-start.4
  184.3 0.8 fusion.94
  185.1 0.8 fusion.93
  186.1 20.1 %all-reduce.4 = (f32[1,1792]{1,0:T(1,128)}, f32[1,28]{1,0:T(1,128)}, f32[1,28]{1,0:T(1,128)}, f32[1,28]{1,0:T(1,128)}) all-reduce(f32[1,1792]{1,0:T(1,128)S(1)} %broadcast_in_dim.73, f32[1,28]{1,0:T(1,128)S(1)} %get-tuple-element.329, f32[1,28]{1,0:T(1,128)S(1)} %get-tuple-element.328, ...), channel_id=1, replica_groups=mesh['section'=2,'seq'=8,'head'=2] {'seq'}, use_global_device_ids=true, to_apply=%region_15.17 | all-reduce | flops 1876 | bytes 15008 | tf_op jit(solution)/shard_map/psum | solution.py:226
  206.2 33.6 %reduce-scatter.5.cloned.1.call-done = bf16[32,1792]{1,0:T(8,128)(2,1)} async-done(((bf16[256,1792]{1,0:T(8,128)(2,1)}), bf16[32,1792]{1,0:T(8,128)(2,1)}) %reduce-scatter.5.cloned.1.call-update) | async-done | bytes 114704 | tf_op jit(solution)/shard_map/reduce_scatter | solution.py:218
  239.9 1.6 bitcast_convert_fusion.2
  241.5 0.8 copy.119
  (107 shorter events, 4.3 us)
Async XLA Ops:
  7.2 19.3 %copy-start.3 = (bf16[1,128,1792]{2,1,0:T(8,128)(2,1)S(1)}, bf16[1,128,1792]{2,1,0:T(8,128)(2,1)}, u32[]{:S(2)}) copy-start(bf16[1,128,1792]{2,1,0:T(8,128)(2,1)} %param.15) | copy-start | bytes 1376260
  7.2 45.6 %reduce-scatter.3.cloned.1.call-start = ((), (), s32[]{:S(2)}) async-start(), calls=%async_computation.2 | async-start | bytes 98304 | tf_op jit(solution)/shard_map/reduce_scatter | solution.py:161
  7.2 6.4 %collective-permute-start = (bf16[32,1792]{1,0:T(8,128)(2,1)}, bf16[32,1792]{1,0:T(8,128)(2,1)S(1)}, u32[]{:S(2)}, u32[]{:S(2)}) collective-permute-start(bf16[32,1792]{1,0:T(8,128)(2,1)} %bitcast.251), channel_id=1, source_target_pairs={{0,2},{2,0},{4,6},{6,4},{8,10},{10,8},{12,14},{14,12},{1,3},{3,1},... | collective-permute-start | bytes 344072 | tf_op jit(solution)/shard_map/ppermute | solution.py:155
  10.3 16.6 %copy-start.13 = (f32[1,28]{1,0:T(1,128)S(1)}, f32[1,28]{1,0:T(1,128)}, u32[]{:S(2)}) copy-start(f32[1,28]{1,0:T(1,128)} %param.19) | copy-start | bytes 340
  10.3 16.6 %copy-start.9 = (s32[1,128]{1,0:T(1,128)S(1)}, s32[1,128]{1,0:T(1,128)}, u32[]{:S(2)}) copy-start(s32[1,128]{1,0:T(1,128)} %param.14) | copy-start | bytes 1540
  10.3 34.6 %copy-start.1 = (bf16[1,128,1792]{2,1,0:T(8,128)(2,1)S(1)}, bf16[1,128,1792]{2,1,0:T(8,128)(2,1)}, u32[]{:S(2)}) copy-start(bf16[1,128,1792]{2,1,0:T(8,128)(2,1)} %param.13) | copy-start | bytes 1376260
  14.6 9.1 %collective-permute-start.1 = (bf16[64,1792]{1,0:T(8,128)(2,1)S(1)}, bf16[64,1792]{1,0:T(8,128)(2,1)S(1)}, u32[]{:S(2)}, u32[]{:S(2)}) collective-permute-start(bf16[64,1792]{1,0:T(8,128)(2,1)S(1)} %maximum_select_fusion.2), channel_id=1, source_target_pairs={{0,4},{2,6},{4,0},{6,2},{8,12},{10,14},{12,8},{14,10},{1,5},{3,7},... | collective-permute-start | bytes 688136 | tf_op jit(solution)/shard_map/ppermute | solution.py:155
  17.7 9.1 %collective-permute-start.3 = (s32[1]{0:T(128)}, s32[1]{0:T(128)}, u32[]{:S(2)}, u32[]{:S(2)}) collective-permute-start(s32[1]{0:T(128)} %bitcast.18), channel_id=1, source_target_pairs={{0,2},{2,4},{4,6},{6,8},{8,10},{10,12},{12,14},{1,3},{3,5},{5,7},{... | collective-permute-start | bytes 20 | tf_op jit(solution)/shard_map/ppermute | solution.py:12
  23.8 22.1 %copy-start.4 = (bf16[128,1792]{1,0:T(8,128)(2,1)}, bf16[128,1792]{1,0:T(8,128)(2,1)S(1)}, u32[]{:S(2)}) copy-start(bf16[128,1792]{1,0:T(8,128)(2,1)S(1)} %maximum_select_fusion.1) | copy-start | bytes 1376260
  23.8 21.0 %collective-permute-start.2 = (bf16[128,1792]{1,0:T(8,128)(2,1)S(1)}, bf16[128,1792]{1,0:T(8,128)(2,1)S(1)}, u32[]{:S(2)}, u32[]{:S(2)}) collective-permute-start(bf16[128,1792]{1,0:T(8,128)(2,1)S(1)} %maximum_select_fusion.1), channel_id=1, source_target_pairs={{0,8},{2,10},{4,12},{6,14},{8,0},{10,2},{12,4},{14,6},{1,9},{3,11}... | collective-permute-start | bytes 1376264 | tf_op jit(solution)/shard_map/ppermute | solution.py:155
  26.9 19.1 %copy-start.19 = (f32[28]{0:T(128)}, f32[28]{0:T(128)S(1)}, u32[]{:S(2)}) copy-start(f32[28]{0:T(128)S(1)} %negate_bitcast_fusion) | copy-start | bytes 340
  28.1 17.9 %copy-start.15 = (f32[128]{0:T(128)}, f32[128]{0:T(128)S(1)}, u32[]{:S(2)}) copy-start(f32[128]{0:T(128)S(1)} %get-tuple-element.323) | copy-start | bytes 1540
  28.1 17.9 %copy-start.10 = (f32[1,28]{1,0:T(1,128)S(1)}, f32[1,28]{1,0:T(1,128)}, u32[]{:S(2)}) copy-start(f32[1,28]{1,0:T(1,128)} %param.18) | copy-start | bytes 340
  44.9 1.1 copy-start.17
  45.9 9.7 %copy-start.18 = (f32[1,28]{1,0:T(1,128)S(1)}, f32[1,28]{1,0:T(1,128)}, u32[]{:S(2)}) copy-start(f32[1,28]{1,0:T(1,128)} %param.20) | copy-start | bytes 340
  45.9 60.2 %all-gather.6.cloned.1.call-start = ((), (), s32[]{:S(2)}) async-start(), calls=%async_computation.4 | async-start | bytes 2359296 | tf_op jit(solution)/shard_map/all_gather | solution.py:41
  54.4 25.7 %copy-start.6 = (bf16[128,128]{0,1:T(8,128)(2,1)S(1)}, bf16[128,128]{0,1:T(8,128)(2,1)}, u32[]{:S(2)}) copy-start(bf16[128,128]{0,1:T(8,128)(2,1)} %reduce-scatter.3.cloned.1.call-done) | copy-start | bytes 98308
  55.5 100.6 %all-gather.4.cloned.1.call-start = ((), (), s32[]{:S(2)}) async-start(), calls=%async_computation.3 | async-start | bytes 2359296 | tf_op jit(solution)/shard_map/all_gather | solution.py:18
  83.4 156.4 %reduce-scatter.5.cloned.1.call-start = ((), (), s32[]{:S(2)}) async-start(), calls=%async_computation.5 | async-start | bytes 1032192 | tf_op jit(solution)/shard_map/reduce_scatter | solution.py:218
  166.2 1.7 copy-start.7
  166.2 1.7 copy-start.8
  172.8 3.5 %copy-start.2 = (bf16[1,128,1792]{2,1,0:T(8,128)(2,1)S(1)}, bf16[1,128,1792]{2,1,0:T(8,128)(2,1)}, u32[]{:S(2)}) copy-start(bf16[1,128,1792]{2,1,0:T(8,128)(2,1)} %param.13) | copy-start | bytes 1376260
  173.0 4.7 %copy-start.11 = (f32[28]{0:T(128)S(1)}, f32[28]{0:T(128)}, u32[]{:S(2)}) copy-start(f32[28]{0:T(128)} %multiply_reduce_fusion.2) | copy-start | bytes 340
  174.0 4.0 %copy-start.16 = (f32[128]{0:T(128)S(1)}, f32[128]{0:T(128)}, u32[]{:S(2)}) copy-start(f32[128]{0:T(128)} %copy-done.15) | copy-start | bytes 1540
  174.0 4.0 %copy-start.20 = (f32[28]{0:T(128)S(1)}, f32[28]{0:T(128)}, u32[]{:S(2)}) copy-start(f32[28]{0:T(128)} %copy-done.19) | copy-start | bytes 340
  174.0 4.4 %copy-start.21 = (f32[28]{0:T(128)S(1)}, f32[28]{0:T(128)}, u32[]{:S(2)}) copy-start(f32[28]{0:T(128)} %add_bitcast_fusion.1) | copy-start | bytes 340
  178.4 1.0 copy-start
  179.5 1.0 copy-start.5
  180.5 5.6 %copy-start.14 = (f32[1,28]{1,0:T(1,128)S(1)}, f32[1,28]{1,0:T(1,128)}, u32[]{:S(2)}) copy-start(f32[1,28]{1,0:T(1,128)} %param.19) | copy-start | bytes 340
  180.5 5.6 %copy-start.12 = (f32[28]{0:T(128)S(1)}, f32[28]{0:T(128)}, u32[]{:S(2)}) copy-start(f32[28]{0:T(128)} %reduce_sum.161) | copy-start | bytes 340
  182.9 23.4 %collective-permute-start.4 = (bf16[1,128,1792]{2,1,0:T(8,128)(2,1)}, bf16[1,128,1792]{2,1,0:T(8,128)(2,1)S(1)}, u32[]{:S(2)}, u32[]{:S(2)}) collective-permute-start(bf16[1,128,1792]{2,1,0:T(8,128)(2,1)} %fusion.3), channel_id=1, source_target_pairs={{16,0},{17,1},{18,2},{19,3},{20,4},{21,5},{22,6},{23,7},{24,8},{25... | collective-permute-start | bytes 1376264 | tf_op jit(solution)/shard_map/ppermute | solution.py:12
Sparse Core Ops, SparseCore 0:
  46.1 6.7 reduce-scatter.2
  55.6 50.4 all-gather.5
  108.3 47.7 all-gather.3
  177.8 61.9 reduce-scatter.4
